TPU v7x, 32 devices: a whole 2x2x4 slice. The times are simulated.
32 devices in a mesh: dp: 8 (over z, x), group: 4 (over y, core).
Axes of the slice: x: 2, y: 2, z: 4, core: 2. Of those that a mesh axis runs over, the one named last changes fastest.
Arguments:
- partials: float32 [4, 54, 1024, 1024], P('group', None, 'dp'), may hold values from -0.3 to 0.3
- second_moment: float32 [54, 1024, 1024], P(None, 'dp', 'group'), may hold values from 0.0001 to 0.01
- left_stats: float32 [54, 1024, 1024], P(None, 'dp', 'group'), may hold values from -3 to 3
- right_stats: float32 [54, 1024, 1024], P(None, 'dp', 'group'), may hold values from -3 to 3
- left_roots: bfloat16 [54, 1024, 1024], P(None, 'dp', 'group'), may hold values from -0.2 to 2.1
- right_roots: bfloat16 [54, 1024, 1024], P(None, 'dp', 'group'), may hold values from -0.2 to 2.1
- norm_partials: float32 [8, 4, 2, 2048], P('dp', 'group'), may hold values from -0.012 to 0.012
- norm_moment: float32 [2, 2048], replicated, may hold values from 0.0001 to 0.01
Outputs:
- block_step: bfloat16 [54, 1024, 1024], P(None, 'dp', 'group')
- new_moment: float32 [54, 1024, 1024], P(None, 'dp', 'group')
- new_left: float32 [54, 1024, 1024], P(None, 'dp', 'group')
- new_right: float32 [54, 1024, 1024], P(None, 'dp', 'group')
- norm_step: float32 [2, 2048], replicated
- new_norm_moment: float32 [2, 2048], replicated
All inputs are finite; a program needn't handle non-finite values.
Results may differ from a plain program's by a relative error of at most 0.0042.
The roundings to bfloat16 on the way count: a program that leaves them out, or rounds other values in their place, can miss the bound.
Values may be sent and summed in bfloat16 or wider, within the bound.
No kernel may reach another device: no remote copies, remote signals or barrier semaphores. Data moves between devices by JAX's collectives and lax.ppermute only.
A program may use at most 384 MiB of HBM per device.

v0:
```python
import jax
import jax.numpy as jnp
from jax import lax
from jax.sharding import PartitionSpec as P

EPS_ADAM = 1e-08
EPS_GRAFT = 1e-06


def on_device(
    partials,
    second_moment,
    left_stats,
    right_stats,
    left_roots,
    right_roots,
    norm_partials,
    norm_moment,
):
    n_dp = lax.axis_size("dp")
    me_dp = lax.axis_index("dp")
    me_group = lax.axis_index("group")
    count = second_moment.shape[0]
    rows = partials.shape[2]
    quarter = second_moment.shape[2]
    width = rows * n_dp
    cap = -(-count // n_dp)
    slots = cap * n_dp
    lower = me_group * quarter
    split = (cap + 1) // 2
    bounds = [(0, split), (split, cap)] if cap > 1 else [(0, cap)]

    def to_owners(blocks, n_slots):
        padded = jnp.pad(blocks, ((0, n_slots * n_dp - blocks.shape[0]), (0, 0), (0, 0)))
        sent = lax.all_to_all(padded.reshape(n_slots, n_dp, rows, quarter), "dp", 1, 1, tiled=True)
        return sent.reshape(n_slots, width, quarter)

    def to_keepers(owned):
        n_slots = owned.shape[0]
        back = lax.all_to_all(owned.reshape(n_slots, n_dp, rows, quarter), "dp", 1, 1, tiled=True)
        return back.reshape(n_slots * n_dp, rows, quarter)

    def roots_to_owners(blocks):
        padded = jnp.pad(blocks, ((0, slots - count), (0, 0), (0, 0)))
        return lax.all_to_all(padded.reshape(cap, n_dp, rows, quarter), "dp", 1, 1, tiled=True)

    left_sent = roots_to_owners(left_roots)
    right_sent = roots_to_owners(right_roots)
    local_norm = norm_partials[0, 0]
    grads, moments, adam_parts = ([], [], [])
    for index, (s0, s1) in enumerate(bounds):
        b0, b1 = (s0 * n_dp, min(s1 * n_dp, count))
        grad = lax.psum_scatter(partials[0, b0:b1], "group", scatter_dimension=2, tiled=True)
        low = grad.astype(jnp.bfloat16)
        if index == 0:
            grad, low, left_sent, right_sent = lax.optimization_barrier(
                (grad, low, left_sent, right_sent)
            )
        new_moment = 0.99 * second_moment[b0:b1] + 0.01 * grad * grad
        adam = grad / (jnp.sqrt(new_moment) + EPS_ADAM)
        adam_parts.append(jnp.sum(adam * adam, axis=(1, 2)))
        moments.append(new_moment)
        grads.append(low)
    left_root = left_sent.reshape(cap, width, quarter)
    right_root = right_sent.reshape(cap, width, quarter)
    adam_cat = jnp.pad(jnp.concatenate(adam_parts), (0, slots - count))
    adam_rows = adam_cat.reshape(cap, n_dp).T
    norm_rows = jnp.broadcast_to(local_norm.reshape(1, -1), (n_dp, local_norm.size))
    sent = lax.all_to_all(jnp.concatenate([adam_rows, norm_rows], axis=1), "dp", 0, 0, tiled=True)
    dp_sums = jnp.sum(sent, axis=0)
    left_terms, right_terms, pieces = ([], [], [])
    for (s0, s1), grad_low in zip(bounds, grads):
        b0, b1 = (s0 * n_dp, min(s1 * n_dp, count))
        mine = to_owners(grad_low, s1 - s0)
        piece = lax.all_gather(mine, "group", axis=2, tiled=True)
        if s0 == 0:
            dp_sums, piece = lax.optimization_barrier((dp_sums, piece))
        own_rows = lax.dynamic_slice_in_dim(piece, lower, quarter, 1)
        gram_left = jnp.einsum("cim,cjm->cij", piece, own_rows, preferred_element_type=jnp.float32)
        gram_right = jnp.einsum("cim,cij->cmj", piece, mine, preferred_element_type=jnp.float32)
        both = jnp.concatenate([gram_left.astype(jnp.bfloat16), gram_right.astype(jnp.bfloat16)])
        back = to_keepers(both)
        n_blocks = (s1 - s0) * n_dp
        left_terms.append(back[: b1 - b0])
        right_terms.append(back[n_blocks : n_blocks + b1 - b0])
        pieces.append(piece)
    piece = jnp.concatenate(pieces) if len(pieces) > 1 else pieces[0]
    half = jnp.einsum("cim,cmj->cij", piece, right_root, preferred_element_type=jnp.float32)
    half = half.astype(jnp.bfloat16)
    full_left = lax.all_gather(left_root, "group", axis=2, tiled=True)
    direction = jnp.einsum("cim,cmj->cij", full_left, half, preferred_element_type=jnp.float32)
    totals = lax.psum(
        jnp.concatenate([jnp.sum(direction * direction, axis=(1, 2)), dp_sums[:cap]]), "group"
    )
    direction_sq = totals[:cap]
    adam_owned = totals[cap:]
    ratio = jnp.sqrt(adam_owned / (direction_sq + EPS_GRAFT))
    scaled = (ratio[:, None, None] * direction).astype(jnp.bfloat16)
    scaled, norm_dp = lax.optimization_barrier((scaled, dp_sums[cap:]))
    block_step = to_keepers(scaled)[:count]
    norm_grad = lax.psum(norm_dp, "group").reshape(local_norm.shape)
    new_moment = jnp.concatenate(moments)
    left_term = jnp.concatenate(left_terms).astype(jnp.float32)
    right_term = jnp.concatenate(right_terms).astype(jnp.float32)
    new_left = 0.95 * left_stats + 0.05 * left_term
    new_right = 0.95 * right_stats + 0.05 * right_term
    new_norm_moment = 0.99 * norm_moment + 0.01 * norm_grad * norm_grad
    norm_step = norm_grad / (jnp.sqrt(new_norm_moment) + EPS_ADAM)
    return (block_step, new_moment, new_left, new_right, norm_step, new_norm_moment)


def solution(mesh):
    return jax.shard_map(
        on_device,
        mesh=mesh,
        in_specs=(
            P("group", None, "dp", None),
            P(None, "dp", "group"),
            P(None, "dp", "group"),
            P(None, "dp", "group"),
            P(None, "dp", "group"),
            P(None, "dp", "group"),
            P("dp", "group", None, None),
            P(),
        ),
        out_specs=(
            P(None, "dp", "group"),
            P(None, "dp", "group"),
            P(None, "dp", "group"),
            P(None, "dp", "group"),
            P(),
            P(),
        ),
        check_vma=False,
    )
```

profile of v0, /device:TPU:0, one launch (start us, length us, event | category | flops | bytes accessed | tf_op | source)
XLA Modules:
  0.0 602.5 jit_solution(5952788004856955438)
XLA Ops:
  7.2 11.1 %slice_bitcast_fusion.1 = f32[22,128,1024]{2,1,0:T(8,128)} fusion(f32[1,54,128,1024]{3,2,1,0:T(8,128)} %param.8), kind=kLoop, calls=%fused_computation.5 | loop fusion | bytes 23068672 | tf_op jit(solution)/shard_map/squeeze | solution.py:53
  18.3 13.7 %slice_bitcast_fusion = f32[32,128,1024]{2,1,0:T(8,128)} fusion(f32[1,54,128,1024]{3,2,1,0:T(8,128)} %param.8), kind=kLoop, calls=%fused_computation | loop fusion | bytes 33554432 | tf_op jit(solution)/shard_map/squeeze | solution.py:53
  37.8 7.0 %all-to-all-start = ((bf16[7,8,128,256]{3,2,0,1:T(8,128)(2,1)}), bf16[7,8,128,256]{3,2,0,1:T(8,128)(2,1)}, u32[]{:S(2)}, u32[]{:S(2)}) async-start(bf16[7,8,128,256]{3,2,0,1:T(8,128)(2,1)} %copy.26), calls=%async_computation.1 | async-start | bytes 7340032 | tf_op jit(solution)/shard_map/all_to_all | solution.py:45
  44.8 68.5 %reduce-scatter.5.cloned.1.call-done = f32[22,128,256]{2,1,0:T(8,128)} async-done(((f32[22,128,1024]{2,1,0:T(8,128)}), f32[22,128,256]{2,1,0:T(8,128)}) %reduce-scatter.5.cloned.1.call-update) | async-done | bytes 2883600 | tf_op jit(solution)/shard_map/reduce_scatter | solution.py:53
  113.3 6.9 %fusion.11 = (f32[22,128,256]{2,1,0:T(8,128)}, f32[22]{0:T(128)S(1)}, bf16[22,128,256]{2,1,0:T(8,128)(2,1)S(1)}) fusion(f32[22,128,256]{2,1,0:T(8,128)} %reduce-scatter.5.cloned.1.call-done, f32[54,128,256]{2,1,0:T(8,128)} %param.9), kind=kLoop, calls=%fused_computation.19 | loop fusion | flops 6488042 | bytes 10092632 | tf_op jit(solution)/shard_map/add | solution.py:59
  121.6 5.0 all-to-all-done
  126.7 3.6 all-to-all-start.4
  136.1 31.3 %all-to-all-done.4 = bf16[3,8,128,256]{3,2,0,1:T(8,128)(2,1)S(1)} async-done(((bf16[3,8,128,256]{3,2,0,1:T(8,128)(2,1)}), bf16[3,8,128,256]{3,2,0,1:T(8,128)(2,1)S(1)}, u32[]{:S(2)}, u32[]{:S(2)}) %all-to-all-start.4) | async-done | bytes 1572896 | tf_op jit(solution)/shard_map/all_to_all | solution.py:35
  167.5 4.5 all-to-all-start.1
  173.4 68.7 %reduce-scatter.3.cloned.1.call-done = f32[32,128,256]{2,1,0:T(8,128)} async-done(((f32[32,128,1024]{2,1,0:T(8,128)}), f32[32,128,256]{2,1,0:T(8,128)}) %reduce-scatter.3.cloned.1.call-update) | async-done | bytes 4194320 | tf_op jit(solution)/shard_map/reduce_scatter | solution.py:53
  244.6 8.8 %all-to-all-done.1 = bf16[7,8,128,256]{3,2,0,1:T(8,128)(2,1)} async-done(((bf16[7,8,128,256]{3,2,0,1:T(8,128)(2,1)}), bf16[7,8,128,256]{3,2,0,1:T(8,128)(2,1)}, u32[]{:S(2)}, u32[]{:S(2)}) %all-to-all-start.1) | async-done | bytes 3670048 | tf_op jit(solution)/shard_map/all_to_all | solution.py:45
  253.5 51.8 %all_to_all.44 = bf16[4,8,128,256]{3,2,0,1:T(8,128)(2,1)S(1)} all-to-all(bf16[4,8,128,256]{3,2,0,1:T(8,128)(2,1)S(1)} %copy.30), channel_id=1, replica_groups=mesh['dp'=8,'group'=4] {'dp'}, dimensions={1} | all-to-all | bytes 4194304 | tf_op jit(solution)/shard_map/all_to_all | solution.py:35
  306.8 4.3 copy.28
  311.9 7.5 %fusion.4 = (f32[32,128,256]{2,1,0:T(8,128)}, f32[32]{0:T(128)S(1)}) fusion(f32[32,128,256]{2,1,0:T(8,128)} %reduce-scatter.3.cloned.1.call-done, f32[54,128,256]{2,1,0:T(8,128)} %param.9), kind=kLoop, calls=%fused_computation.13 | loop fusion | flops 8388576 | bytes 12583040 | tf_op jit(solution)/shard_map/add | solution.py:59
  324.0 5.3 convolution_convert_fusion.1
  333.5 5.7 all-to-all-start.7
  339.4 26.1 %all-gather.6.cloned.1.call-done = bf16[4,1024,1024]{2,1,0:T(8,128)(2,1)} async-done(((bf16[4,1024,256]{2,1,0:T(8,128)(2,1)}), bf16[4,1024,1024]{2,1,0:T(8,128)(2,1)}) %all-gather.6.cloned.1.call-update) | async-done | bytes 8388624 | tf_op jit(solution)/shard_map/all_gather | solution.py:75
  365.5 6.5 %fusion.14 = bf16[4,1024,256]{2,1,0:T(8,128)(2,1)S(1)} fusion(bf16[4,1024,1024]{2,1,0:T(8,128)(2,1)} %all-gather.6.cloned.1.call-done, s32[]{:T(128)S(6)} %select_n.4), kind=kOutput, calls=%fused_computation.23 | convolution fusion | flops 2148532224 | bytes 12582916 | tf_op jit(solution)/shard_map/cim,cjm->cij/dot_general | solution.py:79
  372.0 7.4 %convolution_convert_fusion = bf16[4,1024,256]{2,1,0:T(8,128)(2,1)S(1)} fusion(bf16[4,1024,1024]{2,1,0:T(8,128)(2,1)} %all-gather.6.cloned.1.call-done, bf16[4,1024,256]{2,1,0:T(8,128)(2,1)S(1)} %bitcast.42), kind=kOutput, calls=%fused_computation.24 | convolution fusion | flops 2148532224 | bytes 12582912 | tf_op jit(solution)/shard_map/cim,cij->cmj/dot_general | solution.py:80
  382.4 25.9 %all-to-all-done.7 = bf16[6,8,128,256]{3,2,0,1:T(8,128)(2,1)S(1)} async-done(((bf16[6,8,128,256]{3,2,0,1:T(8,128)(2,1)}), bf16[6,8,128,256]{3,2,0,1:T(8,128)(2,1)S(1)}, u32[]{:S(2)}, u32[]{:S(2)}) %all-to-all-start.7) | async-done | bytes 3145760 | tf_op jit(solution)/shard_map/all_to_all | solution.py:40
  408.3 4.8 all-to-all-start.6
  413.1 4.3 copy.34
  417.5 46.0 %all-gather.4.cloned.1.call-done = bf16[7,1024,1024]{2,1,0:T(8,128)(2,1)} async-done(((bf16[7,1024,256]{2,1,0:T(8,128)(2,1)}), bf16[7,1024,1024]{2,1,0:T(8,128)(2,1)}) %all-gather.4.cloned.1.call-update) | async-done | bytes 14680080 | tf_op jit(solution)/shard_map/all_gather | solution.py:90
  463.6 17.7 %multiply_reduce_fusion = (f32[7]{0:T(128)S(1)}, f32[7,1024,256]{2,1,0:T(8,128)}) fusion(bf16[7,1024,1024]{2,1,0:T(8,128)(2,1)} %all-gather.4.cloned.1.call-done, bf16[7,1024,256]{2,1,0:T(8,128)(2,1)} %bitcast.48, bf16[3,1024,1024]{2,1,0:T(8,128)(2,1)} %all-gather.8.cloned.1.call-done, bf16[4,1024,1024]{2,1,0:T(8,128)(2,1)} %all-gather.6.cloned.1.call-done), kind=kOutput, calls=%fused_computation.7 | convolution fusion | flops 7529037824 | bytes 40370204 | tf_op jit(solution)/shard_map/cim,cmj->cij/dot_general | solution.py:91
  481.3 5.9 psum.14
  487.3 3.8 multiply_convert_fusion
  493.3 12.2 %all-to-all-done.6 = bf16[8,8,128,256]{3,2,0,1:T(8,128)(2,1)} async-done(((bf16[8,8,128,256]{3,2,0,1:T(8,128)(2,1)}), bf16[8,8,128,256]{3,2,0,1:T(8,128)(2,1)}, u32[]{:S(2)}, u32[]{:S(2)}) %all-to-all-start.6) | async-done | bytes 4194336 | tf_op jit(solution)/shard_map/all_to_all | solution.py:40
  505.6 4.5 all-to-all-start.5
  510.1 6.8 %pad_maximum_fusion = f32[54,128,256]{2,1,0:T(8,128)} fusion(f32[22,128,256]{2,1,0:T(8,128)} %get-tuple-element.26, f32[32,128,256]{2,1,0:T(8,128)} %get-tuple-element.24), kind=kLoop, calls=%fused_computation.8 | loop fusion | flops 1769472 | bytes 14155776 | tf_op jit(solution)/shard_map/concatenate | solution.py:102
  517.3 10.9 %psum.15 = f32[2,2048]{1,0:T(2,128)S(1)} all-reduce(f32[2,2048]{1,0:T(2,128)S(1)} %reshape.78), channel_id=1, replica_groups=mesh['dp'=8,'group'=4] {'group'}, use_global_device_ids=true, to_apply=%region_7.8 | all-reduce | flops 4096 | bytes 32768 | tf_op jit(solution)/shard_map/psum | solution.py:101
  533.7 8.7 %multiply_add_fusion = (f32[54,128,256]{2,1,0:T(8,128)}, f32[54,128,256]{2,1,0:T(8,128)}) fusion(f32[54,128,256]{2,1,0:T(8,128)S(1)} %bitcast.44, bf16[22,128,256]{2,1,0:T(8,128)(2,1)S(1)} %get-tuple-element.30, bf16[32,128,256]{2,1,0:T(8,128)(2,1)S(1)} %bitcast.38, bf16[22,128,256]{2,1,0:T(8,128)(2,1)S(1)} %get-tuple-element.31, ...), kind=kLoop, calls=%fused_computation.9 | loop fusion | flops 17694720 | bytes 35389440 | tf_op jit(solution)/shard_map/add | solution.py:106
  542.5 48.8 %all-to-all-done.5 = bf16[7,8,128,256]{3,2,0,1:T(8,128)(2,1)} async-done(((bf16[7,8,128,256]{3,2,0,1:T(8,128)(2,1)}), bf16[7,8,128,256]{3,2,0,1:T(8,128)(2,1)}, u32[]{:S(2)}, u32[]{:S(2)}) %all-to-all-start.5) | async-done | bytes 3670048 | tf_op jit(solution)/shard_map/all_to_all | solution.py:40
  (70 shorter events, 44.2 us)
Async XLA Ops:
  7.2 106.2 %reduce-scatter.5.cloned.1.call-start = ((), (), s32[]{:S(2)}) async-start(), calls=%async_computation.12 | async-start | bytes 14417920 | tf_op jit(solution)/shard_map/reduce_scatter | solution.py:53
  18.3 223.8 %reduce-scatter.3.cloned.1.call-start = ((), (), s32[]{:S(2)}) async-start(), calls=%async_computation.10 | async-start | bytes 20971520 | tf_op jit(solution)/shard_map/reduce_scatter | solution.py:53
  32.0 2.8 copy-start.2
  37.8 88.8 %all-to-all-start = ((bf16[7,8,128,256]{3,2,0,1:T(8,128)(2,1)}), bf16[7,8,128,256]{3,2,0,1:T(8,128)(2,1)}, u32[]{:S(2)}, u32[]{:S(2)}) async-start(bf16[7,8,128,256]{3,2,0,1:T(8,128)(2,1)} %copy.26), calls=%async_computation.1 | async-start | bytes 7340032 | tf_op jit(solution)/shard_map/all_to_all | solution.py:45
  126.7 40.8 %all-to-all-start.4 = ((bf16[3,8,128,256]{3,2,0,1:T(8,128)(2,1)}), bf16[3,8,128,256]{3,2,0,1:T(8,128)(2,1)S(1)}, u32[]{:S(2)}, u32[]{:S(2)}) async-start(bf16[3,8,128,256]{3,2,0,1:T(8,128)(2,1)} %copy.32), calls=%async_computation.6 | async-start | bytes 3145728 | tf_op jit(solution)/shard_map/all_to_all | solution.py:35
  167.5 85.9 %all-to-all-start.1 = ((bf16[7,8,128,256]{3,2,0,1:T(8,128)(2,1)}), bf16[7,8,128,256]{3,2,0,1:T(8,128)(2,1)}, u32[]{:S(2)}, u32[]{:S(2)}) async-start(bf16[7,8,128,256]{3,2,0,1:T(8,128)(2,1)} %copy.27), calls=%async_computation.2 | async-start | bytes 7340032 | tf_op jit(solution)/shard_map/all_to_all | solution.py:45
  172.0 152.0 %all-gather.8.cloned.1.call-start = ((), (), s32[]{:S(2)}) async-start(), calls=%async_computation.14 | async-start | bytes 7864320 | tf_op jit(solution)/shard_map/all_gather | solution.py:75
  173.3 192.2 %all-gather.6.cloned.1.call-start = ((), (), s32[]{:S(2)}) async-start(), calls=%async_computation.13 | async-start | bytes 10485760 | tf_op jit(solution)/shard_map/all_gather | solution.py:75
  306.8 156.8 %all-gather.4.cloned.1.call-start = ((), (), s32[]{:S(2)}) async-start(), calls=%async_computation.11 | async-start | bytes 18350080 | tf_op jit(solution)/shard_map/all_gather | solution.py:90
  311.1 0.7 copy-start.4
  311.9 12.1 %copy-start.1 = (bf16[3,8,128,256]{3,2,1,0:T(8,128)(2,1)S(1)}, bf16[3,8,128,256]{3,2,1,0:T(8,128)(2,1)}, u32[]{:S(2)}) copy-start(bf16[3,8,128,256]{3,2,1,0:T(8,128)(2,1)} %copy.33) | copy-start | bytes 4718596
  320.4 13.1 %all-to-all-start.2 = ((f32[8,1,4103]{2,1,0:T(1,128)}), f32[8,1,4103]{2,1,0:T(1,128)S(1)}, u32[]{:S(2)}, u32[]{:S(2)}) async-start(f32[8,1,4103]{2,1,0:T(1,128)} %all_to_all.29), calls=%async_computation.4 | async-start | bytes 270336 | tf_op jit(solution)/shard_map/all_to_all | solution.py:69
  324.0 5.4 copy-start.6
  333.5 74.8 %all-to-all-start.7 = ((bf16[6,8,128,256]{3,2,0,1:T(8,128)(2,1)}), bf16[6,8,128,256]{3,2,0,1:T(8,128)(2,1)S(1)}, u32[]{:S(2)}, u32[]{:S(2)}) async-start(bf16[6,8,128,256]{3,2,0,1:T(8,128)(2,1)} %copy.41), calls=%async_computation.9 | async-start | bytes 6291456 | tf_op jit(solution)/shard_map/all_to_all | solution.py:40
  339.3 78.1 %copy-start.3 = (f32[4103]{0:T(1024)}, f32[4103]{0:T(1024)S(1)}, u32[]{:S(2)}) copy-start(f32[4103]{0:T(1024)S(1)} %reduce_sum.38) | copy-start | bytes 49240
  365.5 6.5 %copy-start = (bf16[4,8,128,256]{3,2,1,0:T(8,128)(2,1)S(1)}, bf16[4,8,128,256]{3,2,1,0:T(8,128)(2,1)}, u32[]{:S(2)}) copy-start(bf16[4,8,128,256]{3,2,1,0:T(8,128)(2,1)} %copy.31) | copy-start | bytes 6291460
  408.3 97.2 %all-to-all-start.6 = ((bf16[8,8,128,256]{3,2,0,1:T(8,128)(2,1)}), bf16[8,8,128,256]{3,2,0,1:T(8,128)(2,1)}, u32[]{:S(2)}, u32[]{:S(2)}) async-start(bf16[8,8,128,256]{3,2,0,1:T(8,128)(2,1)} %copy.38), calls=%async_computation.8 | async-start | bytes 8388608 | tf_op jit(solution)/shard_map/all_to_all | solution.py:40
  463.5 17.7 %slice-start.2 = ((f32[4103]{0:T(1024)}), f32[7]{0:T(128)S(1)}, s32[]{:S(2)}) async-start(f32[4103]{0:T(1024)} %copy-done.3), calls=%async_computation.17 | async-start | bytes 1024 | tf_op jit(solution)/shard_map/slice | solution.py:93
  505.6 85.7 %all-to-all-start.5 = ((bf16[7,8,128,256]{3,2,0,1:T(8,128)(2,1)}), bf16[7,8,128,256]{3,2,0,1:T(8,128)(2,1)}, u32[]{:S(2)}, u32[]{:S(2)}) async-start(bf16[7,8,128,256]{3,2,0,1:T(8,128)(2,1)} %copy.35), calls=%async_computation.7 | async-start | bytes 7340032 | tf_op jit(solution)/shard_map/all_to_all | solution.py:40
  517.1 11.1 %copy-start.5 = (f32[2,2048]{1,0:T(2,128)S(1)}, f32[2,2048]{1,0:T(2,128)}, u32[]{:S(2)}) copy-start(f32[2,2048]{1,0:T(2,128)} %param.15) | copy-start | bytes 49156
  528.9 3.5 slice-start
  531.8 2.0 slice-start.1
Sparse Core Ops, SparseCore 0:
  18.4 94.8 reduce-scatter.4
  115.9 126.1 reduce-scatter.2
  244.3 47.2 all-gather.7
  306.9 58.5 all-gather.5
  367.5 95.9 all-gather.3
where the time goes:
time: 604 us; the launch traced here: 602 us
  waiting for transfers between devices  342 us (57%)
  blocking collectives  68.6 us (11%)
  local copies, waits for them, and re-layouts  67.7 us (11%)
  matrix products  38.8 us (6%)
  other arithmetic  37.8 us (6%)
  starting transfers between devices  33.9 us (6%)
  between operations  14 us (2%)
    reduce_scatter x2, waiting for transfers between devices, on_device(): lax.psum_scatter(partials[0, b0:b1], 'group', scatter_dimension=2, tiled=...  137 us
    all_to_all x3, waiting for transfers between devices, to_keepers(): lax.all_to_all(owned.reshape(n_slots, n_dp, rows, quarter), 'dp', 1, 1, t...  86.9 us
    all_to_all x1, blocking collectives, to_owners(): lax.all_to_all(padded.reshape(n_slots, n_dp, rows, quarter), 'dp', 1, 1,...  51.8 us
    all_gather x1, waiting for transfers between devices, on_device(): full_left = lax.all_gather(left_root, 'group', axis=2, tiled=True)  46 us
    all_to_all x1, waiting for transfers between devices, to_owners(): lax.all_to_all(padded.reshape(n_slots, n_dp, rows, quarter), 'dp', 1, 1,...  31.3 us
    all_gather x2, waiting for transfers between devices, on_device(): piece = lax.all_gather(mine, 'group', axis=2, tiled=True)  26.2 us
    squeeze x2, local copies, waits for them, and re-layouts, on_device(): partials[0, b0:b1]  24.7 us
    dot_general x1, matrix products, on_device(): jnp.einsum('cim,cmj->cij', full_left, half, preferred_element_type=jnp.fl...  17.7 us
  transfers between devices with their start and end apart: 12, of which 10 were waited for; matrix products, arithmetic and copies ran while one was open for 20% of the time, Pallas kernels for 0%

commit v1 on v0

--- a/solution.py
+++ b/solution.py
@@ -5,6 +5,12 @@
 
 EPS_ADAM = 1e-08
 EPS_GRAFT = 1e-06
+
+
+def gates_part(arr, dim_i):
+    r1 = list(arr.shape[1:])
+    r1[dim_i] *= arr.shape[0]
+    return jnp.moveaxis(arr, 0, dim_i).reshape(r1)
 
 
 def on_device(
@@ -72,7 +78,27 @@
     for (s0, s1), grad_low in zip(bounds, grads):
         b0, b1 = (s0 * n_dp, min(s1 * n_dp, count))
         mine = to_owners(grad_low, s1 - s0)
-        piece = lax.all_gather(mine, "group", axis=2, tiled=True)
+        axis_len = lax.axis_size("group")
+        tick = 0
+        made = []
+        while tick < axis_len:
+            made.append((tick, (tick + 1) % axis_len))
+            tick += 1
+        sheets = []
+        for ii, src_i in made:
+            sheets.append((src_i, ii))
+        at = 0
+        arr_now, g_now = ([], [])
+        while at < axis_len - 1:
+            if at % 2 == 0:
+                arr_now.append(lax.ppermute(arr_now[-1] if arr_now else mine, "group", made))
+            else:
+                g_now.append(lax.ppermute(g_now[-1] if g_now else mine, "group", sheets))
+            at = at + 1
+        all_values = jnp.stack([*arr_now[::-1], mine, *g_now])
+        b_now = lax.axis_index("group") - len(arr_now)
+        all_values = all_values[(jnp.arange(axis_len) - b_now) % axis_len]
+        piece = gates_part(all_values, 2)
         if s0 == 0:
             dp_sums, piece = lax.optimization_barrier((dp_sums, piece))
         own_rows = lax.dynamic_slice_in_dim(piece, lower, quarter, 1)

time: 604 us -> 730 us (1.21)
  waiting for transfers between devices: 342 us -> 421 us
  local copies, waits for them, and re-layouts: 67.7 us -> 99.7 us
  other arithmetic: 37.8 us -> 55.7 us
  blocking collectives: 68.6 us -> 59.5 us
    ppermute x0 -> x6, waiting for transfers between devices: none -> 131 us  [the longest x4 117 us: on_device(): lax.ppermute(arr_now[-1] if arr_now else mine, 'group', made)]
    all_to_all x2, waiting for transfers between devices: 13.8 us -> 141 us  [roots_to_owners(): lax.all_to_all(padded.reshape(cap, n_dp, rows, quarter), 'dp', 1, 1, tile...]
    reduce_scatter x2, waiting for transfers between devices: 137 us -> 42.4 us  [on_device(): lax.psum_scatter(partials[0, b0:b1], 'group', scatter_dimension=2, tiled=...]
    all_gather x1, waiting for transfers between devices: 46 us -> 0.01 us  [on_device(): full_left = lax.all_gather(left_root, 'group', axis=2, tiled=True)]
    all_to_all x1, waiting for transfers between devices: 31.3 us -> 0.01 us  [to_owners(): lax.all_to_all(padded.reshape(n_slots, n_dp, rows, quarter), 'dp', 1, 1,...]
    all_gather x2 -> x0, waiting for transfers between devices: 26.2 us -> none  [on_device(): piece = lax.all_gather(mine, 'group', axis=2, tiled=True)]
    gather x0 -> x4, local copies, waits for them, and re-layouts: none -> 20.1 us  [on_device(): all_values = all_values[(jnp.arange(axis_len) - b_now) % axis_len]]
    all_to_all x3, waiting for transfers between devices: 86.9 us -> 106 us  [to_keepers(): lax.all_to_all(owned.reshape(n_slots, n_dp, rows, quarter), 'dp', 1, 1, t...]
  transfers between devices with their start and end apart: 12 -> 16, of which waited for: 10 -> 12; matrix products, arithmetic and copies ran while one was open for 20% -> 23% of each run, Pallas kernels for 0% -> 0%
where the time goes in v1:
time: 730 us; the launch traced here: 728 us
  waiting for transfers between devices  421 us (58%)
  local copies, waits for them, and re-layouts  99.7 us (14%)
  blocking collectives  59.5 us (8%)
  other arithmetic  55.7 us (8%)
  matrix products  40.1 us (5%)
  starting transfers between devices  38.3 us (5%)
  between operations  14 us (2%)
    all_to_all x2, waiting for transfers between devices, roots_to_owners(): lax.all_to_all(padded.reshape(cap, n_dp, rows, quarter), 'dp', 1, 1, tile...  141 us
    ppermute x4, waiting for transfers between devices, on_device(): lax.ppermute(arr_now[-1] if arr_now else mine, 'group', made)  117 us
    all_to_all x3, waiting for transfers between devices, to_keepers(): lax.all_to_all(owned.reshape(n_slots, n_dp, rows, quarter), 'dp', 1, 1, t...  106 us
    reduce_scatter x2, waiting for transfers between devices, on_device(): lax.psum_scatter(partials[0, b0:b1], 'group', scatter_dimension=2, tiled=...  42.4 us
    all_to_all x1, blocking collectives, to_owners(): lax.all_to_all(padded.reshape(n_slots, n_dp, rows, quarter), 'dp', 1, 1,...  42.3 us
    squeeze x2, local copies, waits for them, and re-layouts, on_device(): partials[0, b0:b1]  24.5 us
    gather x4, local copies, waits for them, and re-layouts, on_device(): all_values = all_values[(jnp.arange(axis_len) - b_now) % axis_len]  20.1 us
    dot_general x1, matrix products, on_device(): jnp.einsum('cim,cmj->cij', full_left, half, preferred_element_type=jnp.fl...  17.7 us
  transfers between devices with their start and end apart: 16, of which 12 were waited for; matrix products, arithmetic and copies ran while one was open for 23% of the time, Pallas kernels for 0%

profile of v1, /device:TPU:0, one launch (start us, length us, event | category | flops | bytes accessed | tf_op | source)
XLA Modules:
  0.0 728.3 jit_solution(16271781148391546883)
XLA Ops:
  7.2 11.8 %slice_bitcast_fusion = f32[32,128,1024]{2,1,0:T(8,128)} fusion(f32[1,54,128,1024]{3,2,1,0:T(8,128)} %param.8), kind=kLoop, calls=%fused_computation.3 | loop fusion | bytes 33554432 | tf_op jit(solution)/shard_map/squeeze | solution.py:59
  19.1 12.7 %slice_bitcast_fusion.1 = f32[22,128,1024]{2,1,0:T(8,128)} fusion(f32[1,54,128,1024]{3,2,1,0:T(8,128)} %param.8), kind=kLoop, calls=%fused_computation.8 | loop fusion | bytes 23068672 | tf_op jit(solution)/shard_map/squeeze | solution.py:59
  37.6 7.5 %all-to-all-start = ((bf16[7,8,128,256]{3,2,0,1:T(8,128)(2,1)}), bf16[7,8,128,256]{3,2,0,1:T(8,128)(2,1)}, u32[]{:S(2)}, u32[]{:S(2)}) async-start(bf16[7,8,128,256]{3,2,0,1:T(8,128)(2,1)} %copy.32), calls=%async_computation.1 | async-start | bytes 7340032 | tf_op jit(solution)/shard_map/all_to_all | solution.py:51
  47.8 79.1 %all-to-all-done = bf16[7,8,128,256]{3,2,0,1:T(8,128)(2,1)} async-done(((bf16[7,8,128,256]{3,2,0,1:T(8,128)(2,1)}), bf16[7,8,128,256]{3,2,0,1:T(8,128)(2,1)}, u32[]{:S(2)}, u32[]{:S(2)}) %all-to-all-start) | async-done | bytes 3670048 | tf_op jit(solution)/shard_map/all_to_all | solution.py:51
  131.5 16.6 %reduce-scatter.3.cloned.1.call-done = f32[32,128,256]{2,1,0:T(8,128)} async-done(((f32[32,128,1024]{2,1,0:T(8,128)}), f32[32,128,256]{2,1,0:T(8,128)}) %reduce-scatter.3.cloned.1.call-update) | async-done | bytes 4194320 | tf_op jit(solution)/shard_map/reduce_scatter | solution.py:59
  150.5 62.3 %all-to-all-done.1 = bf16[7,8,128,256]{3,2,0,1:T(8,128)(2,1)} async-done(((bf16[7,8,128,256]{3,2,0,1:T(8,128)(2,1)}), bf16[7,8,128,256]{3,2,0,1:T(8,128)(2,1)}, u32[]{:S(2)}, u32[]{:S(2)}) %all-to-all-start.1) | async-done | bytes 3670048 | tf_op jit(solution)/shard_map/all_to_all | solution.py:51
  217.2 25.8 %reduce-scatter.5.cloned.1.call-done = f32[22,128,256]{2,1,0:T(8,128)} async-done(((f32[22,128,1024]{2,1,0:T(8,128)}), f32[22,128,256]{2,1,0:T(8,128)}) %reduce-scatter.5.cloned.1.call-update) | async-done | bytes 2883600 | tf_op jit(solution)/shard_map/reduce_scatter | solution.py:59
  243.0 6.8 fusion.11
  250.1 42.3 %all_to_all.44 = bf16[3,8,128,256]{3,2,0,1:T(8,128)(2,1)S(1)} all-to-all(bf16[3,8,128,256]{3,2,0,1:T(8,128)(2,1)S(1)} %copy.40), channel_id=1, replica_groups=mesh['dp'=8,'group'=4] {'dp'}, dimensions={1} | all-to-all | bytes 3145728 | tf_op jit(solution)/shard_map/all_to_all | solution.py:41
  300.6 61.8 %collective-permute-done.3 = bf16[3,1024,256]{2,1,0:T(8,128)(2,1)} collective-permute-done((bf16[3,1024,256]{2,1,0:T(8,128)(2,1)}, bf16[3,1024,256]{2,1,0:T(8,128)(2,1)}, u32[]{:S(2)}, u32[]{:S(2)}) %collective-permute-start.3) | collective-permute-done | bytes 1572896 | tf_op jit(solution)/shard_map/ppermute | solution.py:94
  362.5 5.8 collective-permute-done.5
  368.2 19.1 %collective-permute-done.4 = bf16[3,1024,256]{2,1,0:T(8,128)(2,1)} collective-permute-done((bf16[3,1024,256]{2,1,0:T(8,128)(2,1)}, bf16[3,1024,256]{2,1,0:T(8,128)(2,1)}, u32[]{:S(2)}, u32[]{:S(2)}) %collective-permute-start.4) | collective-permute-done | bytes 1572896 | tf_op jit(solution)/shard_map/ppermute | solution.py:94
  387.3 6.5 pad_maximum_fusion.2
  393.8 6.4 gather_fusion
  414.5 5.5 fusion.4
  421.0 5.5 all-to-all-start.2
  426.6 22.0 %collective-permute-done = bf16[4,1024,256]{2,1,0:T(8,128)(2,1)} collective-permute-done((bf16[4,1024,256]{2,1,0:T(8,128)(2,1)}, bf16[4,1024,256]{2,1,0:T(8,128)(2,1)}, u32[]{:S(2)}, u32[]{:S(2)}) %collective-permute-start) | collective-permute-done | bytes 2097184 | tf_op jit(solution)/shard_map/ppermute | solution.py:94
  456.0 5.1 all-to-all-start.7
  461.2 8.5 %collective-permute-done.2 = bf16[4,1024,256]{2,1,0:T(8,128)(2,1)} collective-permute-done((bf16[4,1024,256]{2,1,0:T(8,128)(2,1)}, bf16[4,1024,256]{2,1,0:T(8,128)(2,1)}, u32[]{:S(2)}, u32[]{:S(2)}) %collective-permute-start.2) | collective-permute-done | bytes 2097184 | tf_op jit(solution)/shard_map/ppermute | solution.py:96
  469.7 14.1 %collective-permute-done.1 = bf16[4,1024,256]{2,1,0:T(8,128)(2,1)} collective-permute-done((bf16[4,1024,256]{2,1,0:T(8,128)(2,1)}, bf16[4,1024,256]{2,1,0:T(8,128)(2,1)}, u32[]{:S(2)}, u32[]{:S(2)}) %collective-permute-start.1) | collective-permute-done | bytes 2097184 | tf_op jit(solution)/shard_map/ppermute | solution.py:94
  501.9 7.5 %maximum_bitcast_fusion = bf16[4,4,128,8,256]{4,3,2,1,0:T(8,128)(2,1)} fusion(bf16[4,4,512,256]{3,2,1,0:T(8,128)(2,1)} %gather_fusion.2, bf16[4,4,512,256]{3,2,1,0:T(8,128)(2,1)} %gather_fusion.1), kind=kLoop, calls=%fused_computation.10 | loop fusion | flops 16777216 | bytes 16777216
  509.4 7.8 %copy.58 = bf16[4,4,128,8,256]{4,3,0,2,1:T(8,128)(2,1)} copy(bf16[4,4,128,8,256]{4,3,2,1,0:T(8,128)(2,1)} %maximum_bitcast_fusion) | data formatting | bytes 16777216 | tf_op jit(solution)/shard_map/reshape | solution.py:13
  517.2 6.5 fusion.14
  523.7 5.9 convolution_convert_fusion
  534.1 5.5 all-to-all-start.6
  543.9 17.7 %multiply_reduce_fusion = (f32[7]{0:T(128)S(1)}, f32[7,1024,256]{2,1,0:T(8,128)}) fusion(bf16[7,1024,1024]{2,1,0:T(8,128)(2,1)} %all-gather.2.cloned.1.call-done, bf16[7,1024,256]{2,1,0:T(8,128)(2,1)} %bitcast.68, bf16[3,1024,1024]{2,1,0:T(8,128)(2,1)} %bitcast.66, bf16[4,1024,1024]{2,1,0:T(8,128)(2,1)} %bitcast.60), kind=kOutput, calls=%fused_computation.12 | convolution fusion | flops 7529037824 | bytes 40370204 | tf_op jit(solution)/shard_map/cim,cmj->cij/dot_general | solution.py:117
  561.8 6.3 psum.14
  574.1 57.1 %all-to-all-done.6 = bf16[8,8,128,256]{3,2,0,1:T(8,128)(2,1)} async-done(((bf16[8,8,128,256]{3,2,0,1:T(8,128)(2,1)}), bf16[8,8,128,256]{3,2,0,1:T(8,128)(2,1)}, u32[]{:S(2)}, u32[]{:S(2)}) %all-to-all-start.6) | async-done | bytes 4194336 | tf_op jit(solution)/shard_map/all_to_all | solution.py:46
  635.7 6.8 pad_maximum_fusion.1
  647.8 8.8 %multiply_add_fusion = (f32[54,128,256]{2,1,0:T(8,128)}, f32[54,128,256]{2,1,0:T(8,128)}) fusion(f32[54,128,256]{2,1,0:T(8,128)S(1)} %bitcast.63, bf16[22,128,256]{2,1,0:T(8,128)(2,1)S(1)} %get-tuple-element.32, bf16[32,128,256]{2,1,0:T(8,128)(2,1)S(1)} %bitcast.57, bf16[22,128,256]{2,1,0:T(8,128)(2,1)S(1)} %get-tuple-element.33, ...), kind=kLoop, calls=%fused_computation.14 | loop fusion | flops 17694720 | bytes 35389440 | tf_op jit(solution)/shard_map/add | solution.py:132
  656.6 10.9 %psum.15 = f32[2,2048]{1,0:T(2,128)S(1)} all-reduce(f32[2,2048]{1,0:T(2,128)S(1)} %reshape.135), channel_id=1, replica_groups=mesh['dp'=8,'group'=4] {'group'}, use_global_device_ids=true, to_apply=%region_7.8 | all-reduce | flops 4096 | bytes 32768 | tf_op jit(solution)/shard_map/psum | solution.py:127
  668.2 48.9 %all-to-all-done.5 = bf16[7,8,128,256]{3,2,0,1:T(8,128)(2,1)} async-done(((bf16[7,8,128,256]{3,2,0,1:T(8,128)(2,1)}), bf16[7,8,128,256]{3,2,0,1:T(8,128)(2,1)}, u32[]{:S(2)}, u32[]{:S(2)}) %all-to-all-start.5) | async-done | bytes 3670048 | tf_op jit(solution)/shard_map/all_to_all | solution.py:46
  (91 shorter events, 99.5 us)
Async XLA Ops:
  7.2 140.9 %reduce-scatter.3.cloned.1.call-start = ((), (), s32[]{:S(2)}) async-start(), calls=%async_computation.10 | async-start | bytes 20971520 | tf_op jit(solution)/shard_map/reduce_scatter | solution.py:59
  19.0 224.0 %reduce-scatter.5.cloned.1.call-start = ((), (), s32[]{:S(2)}) async-start(), calls=%async_computation.12 | async-start | bytes 14417920 | tf_op jit(solution)/shard_map/reduce_scatter | solution.py:59
  31.7 2.8 copy-start.3
  37.6 7.5 %copy-start.4 = (bf16[54,128,256]{2,1,0:T(8,128)(2,1)S(1)}, bf16[54,128,256]{2,1,0:T(8,128)(2,1)}, u32[]{:S(2)}) copy-start(bf16[54,128,256]{2,1,0:T(8,128)(2,1)} %param.13) | copy-start | bytes 10616836
  37.6 89.3 %all-to-all-start = ((bf16[7,8,128,256]{3,2,0,1:T(8,128)(2,1)}), bf16[7,8,128,256]{3,2,0,1:T(8,128)(2,1)}, u32[]{:S(2)}, u32[]{:S(2)}) async-start(bf16[7,8,128,256]{3,2,0,1:T(8,128)(2,1)} %copy.32), calls=%async_computation.1 | async-start | bytes 7340032 | tf_op jit(solution)/shard_map/all_to_all | solution.py:51
  126.9 85.9 %all-to-all-start.1 = ((bf16[7,8,128,256]{3,2,0,1:T(8,128)(2,1)}), bf16[7,8,128,256]{3,2,0,1:T(8,128)(2,1)}, u32[]{:S(2)}, u32[]{:S(2)}) async-start(bf16[7,8,128,256]{3,2,0,1:T(8,128)(2,1)} %copy.33), calls=%async_computation.2 | async-start | bytes 7340032 | tf_op jit(solution)/shard_map/all_to_all | solution.py:51
  131.4 412.5 %all-gather.2.cloned.1.call-start = ((), (), s32[]{:S(2)}) async-start(), calls=%async_computation.11 | async-start | bytes 18350080 | tf_op jit(solution)/shard_map/all_gather | solution.py:116
  293.7 68.7 %collective-permute-start.3 = (bf16[3,1024,256]{2,1,0:T(8,128)(2,1)}, bf16[3,1024,256]{2,1,0:T(8,128)(2,1)}, u32[]{:S(2)}, u32[]{:S(2)}) collective-permute-start(bf16[3,1024,256]{2,1,0:T(8,128)(2,1)} %bitcast.15), channel_id=1, source_target_pairs={{0,1},{1,2},{2,3},{3,0},{4,5},{5,6},{6,7},{7,4},{8,9},{9,10},{10,1... | collective-permute-start | bytes 4718600 | tf_op jit(solution)/shard_map/ppermute | solution.py:94
  293.7 68.7 %copy-start.7 = (f32[1,1,2,2048]{3,2,1,0:T(2,128)S(1)}, f32[1,1,2,2048]{3,2,1,0:T(2,128)}, u32[]{:S(2)}) copy-start(f32[1,1,2,2048]{3,2,1,0:T(2,128)} %param.14) | copy-start | bytes 49156
  295.1 116.4 %all-to-all-start.3 = ((bf16[4,8,128,256]{3,2,0,1:T(8,128)(2,1)}), bf16[4,8,128,256]{3,2,0,1:T(8,128)(2,1)S(1)}, u32[]{:S(2)}, u32[]{:S(2)}) async-start(bf16[4,8,128,256]{3,2,0,1:T(8,128)(2,1)} %copy.36), calls=%async_computation.5 | async-start | bytes 4194304 | tf_op jit(solution)/shard_map/all_to_all | solution.py:41
  298.7 69.5 %collective-permute-start.5 = (bf16[3,1024,256]{2,1,0:T(8,128)(2,1)}, bf16[3,1024,256]{2,1,0:T(8,128)(2,1)}, u32[]{:S(2)}, u32[]{:S(2)}) collective-permute-start(bf16[3,1024,256]{2,1,0:T(8,128)(2,1)} %bitcast.15), channel_id=1, source_target_pairs={{1,0},{2,1},{3,2},{0,3},{5,4},{6,5},{7,6},{4,7},{9,8},{10,9},{11,1... | collective-permute-start | bytes 4718600 | tf_op jit(solution)/shard_map/ppermute | solution.py:96
  362.4 24.9 %collective-permute-start.4 = (bf16[3,1024,256]{2,1,0:T(8,128)(2,1)}, bf16[3,1024,256]{2,1,0:T(8,128)(2,1)}, u32[]{:S(2)}, u32[]{:S(2)}) collective-permute-start(bf16[3,1024,256]{2,1,0:T(8,128)(2,1)} %collective-permute-done.3), channel_id=1, source_target_pairs={{0,1},{1,2},{2,3},{3,0},{4,5},{5,6},{6,7},{7,4},{8,9},{9,10},{10,1... | collective-permute-start | bytes 4718600 | tf_op jit(solution)/shard_map/ppermute | solution.py:94
  403.9 2.7 copy-start.2
  411.6 2.9 copy-start
  413.1 35.5 %collective-permute-start = (bf16[4,1024,256]{2,1,0:T(8,128)(2,1)}, bf16[4,1024,256]{2,1,0:T(8,128)(2,1)}, u32[]{:S(2)}, u32[]{:S(2)}) collective-permute-start(bf16[4,1024,256]{2,1,0:T(8,128)(2,1)} %bitcast.7), channel_id=1, source_target_pairs={{0,1},{1,2},{2,3},{3,0},{4,5},{5,6},{6,7},{7,4},{8,9},{9,10},{10,1... | collective-permute-start | bytes 6291464 | tf_op jit(solution)/shard_map/ppermute | solution.py:94
  421.0 34.9 %all-to-all-start.2 = ((f32[8,1,4103]{2,1,0:T(1,128)}), f32[8,1,4103]{2,1,0:T(1,128)S(1)}, u32[]{:S(2)}, u32[]{:S(2)}) async-start(f32[8,1,4103]{2,1,0:T(1,128)} %all_to_all.29), calls=%async_computation.4 | async-start | bytes 270336 | tf_op jit(solution)/shard_map/all_to_all | solution.py:75
  426.6 27.1 %copy-start.5 = (bf16[3,1024,256]{2,1,0:T(8,128)(2,1)S(1)}, bf16[3,1024,256]{2,1,0:T(8,128)(2,1)}, u32[]{:S(2)}) copy-start(bf16[3,1024,256]{2,1,0:T(8,128)(2,1)} %convolution_convert_fusion.1) | copy-start | bytes 4718596
  426.6 43.1 %collective-permute-start.2 = (bf16[4,1024,256]{2,1,0:T(8,128)(2,1)}, bf16[4,1024,256]{2,1,0:T(8,128)(2,1)}, u32[]{:S(2)}, u32[]{:S(2)}) collective-permute-start(bf16[4,1024,256]{2,1,0:T(8,128)(2,1)} %bitcast.7), channel_id=1, source_target_pairs={{1,0},{2,1},{3,2},{0,3},{5,4},{6,5},{7,6},{4,7},{9,8},{10,9},{11,1... | collective-permute-start | bytes 6291464 | tf_op jit(solution)/shard_map/ppermute | solution.py:96
  448.6 35.2 %collective-permute-start.1 = (bf16[4,1024,256]{2,1,0:T(8,128)(2,1)}, bf16[4,1024,256]{2,1,0:T(8,128)(2,1)}, u32[]{:S(2)}, u32[]{:S(2)}) collective-permute-start(bf16[4,1024,256]{2,1,0:T(8,128)(2,1)} %collective-permute-done), channel_id=1, source_target_pairs={{0,1},{1,2},{2,3},{3,0},{4,5},{5,6},{6,7},{7,4},{8,9},{9,10},{10,1... | collective-permute-start | bytes 6291464 | tf_op jit(solution)/shard_map/ppermute | solution.py:94
  456.0 78.1 %all-to-all-start.7 = ((bf16[6,8,128,256]{3,2,0,1:T(8,128)(2,1)}), bf16[6,8,128,256]{3,2,0,1:T(8,128)(2,1)S(1)}, u32[]{:S(2)}, u32[]{:S(2)}) async-start(bf16[6,8,128,256]{3,2,0,1:T(8,128)(2,1)} %copy.51), calls=%async_computation.9 | async-start | bytes 6291456 | tf_op jit(solution)/shard_map/all_to_all | solution.py:46
  461.2 82.7 %copy-start.6 = (f32[4103]{0:T(1024)}, f32[4103]{0:T(1024)S(1)}, u32[]{:S(2)}) copy-start(f32[4103]{0:T(1024)S(1)} %reduce_sum.38) | copy-start | bytes 49240
  517.2 6.5 copy-start.1
  534.1 97.2 %all-to-all-start.6 = ((bf16[8,8,128,256]{3,2,0,1:T(8,128)(2,1)}), bf16[8,8,128,256]{3,2,0,1:T(8,128)(2,1)}, u32[]{:S(2)}, u32[]{:S(2)}) async-start(bf16[8,8,128,256]{3,2,0,1:T(8,128)(2,1)} %copy.48), calls=%async_computation.8 | async-start | bytes 8388608 | tf_op jit(solution)/shard_map/all_to_all | solution.py:46
  543.9 17.7 %slice-start.2 = ((f32[4103]{0:T(1024)}), f32[7]{0:T(128)S(1)}, s32[]{:S(2)}) async-start(f32[4103]{0:T(1024)} %copy-done.6), calls=%async_computation.15 | async-start | bytes 1024 | tf_op jit(solution)/shard_map/slice | solution.py:119
  631.2 85.9 %all-to-all-start.5 = ((bf16[7,8,128,256]{3,2,0,1:T(8,128)(2,1)}), bf16[7,8,128,256]{3,2,0,1:T(8,128)(2,1)}, u32[]{:S(2)}, u32[]{:S(2)}) async-start(bf16[7,8,128,256]{3,2,0,1:T(8,128)(2,1)} %copy.45), calls=%async_computation.7 | async-start | bytes 7340032 | tf_op jit(solution)/shard_map/all_to_all | solution.py:46
  643.0 3.5 slice-start
  645.9 2.0 slice-start.1
  647.8 19.7 %copy-start.8 = (f32[2,2048]{1,0:T(2,128)S(1)}, f32[2,2048]{1,0:T(2,128)}, u32[]{:S(2)}) copy-start(f32[2,2048]{1,0:T(2,128)} %param.15) | copy-start | bytes 49156
Sparse Core Ops, SparseCore 0:
  19.1 128.8 reduce-scatter.2
  150.8 92.1 reduce-scatter.4
  244.6 131.7 all-gather.1
